TPU v7x, 128 devices: a whole 4x4x4 slice. The times are simulated.
128 devices in a mesh: seq: 16 (over x_lo, z, core), batch: 8 (over y, x_hi).
Axes of the slice: x: 4 (x_hi: 2, x_lo: 2; x = x_hi * 2 + x_lo), y: 4, z: 4, core: 2. Of those that a mesh axis runs over, the one named last changes fastest.
Arguments:
- activations: bfloat16 [2, 8192, 1536], P(None, ('seq', 'batch')), may hold values from -6 to 6
- conv_gain: float32 [1536], replicated, may hold values from 0.25 to 1.75
- conv_weight: bfloat16 [5, 1536, 1536], P(None, 'batch'), may hold values from -0.0625 to 0.0625
- attention_gain: float32 [1536], replicated, may hold values from 0.25 to 1.75
- query_weight: bfloat16 [1536, 1536], P('batch'), may hold values from -3 to 3
- key_weight: bfloat16 [1536, 1536], P('batch'), may hold values from -3 to 3
- value_weight: bfloat16 [1536, 1536], P('batch'), may hold values from -0.15625 to 0.15625
- output_weight: bfloat16 [1536, 1536], P('batch'), may hold values from -0.15625 to 0.15625
Outputs:
- block_out: bfloat16 [2, 8192, 1536], P(None, ('seq', 'batch'))
All inputs are finite; a program needn't handle non-finite values.
Results may differ from a plain program's by a relative error of at most 0.015.
Values may be sent and summed in bfloat16 or wider, within the bound.
No kernel may reach another device: no remote copies, remote signals or barrier semaphores. Data moves between devices by JAX's collectives and lax.ppermute only.
A program may use at most 128 MiB of HBM per device.

v0:
```python
import math
import jax
import jax.numpy as jnp
from jax import lax
from jax.sharding import PartitionSpec as P

HD = 192


def with_halo(cells, sides, width):
    for axis, dim in sides:
        count = lax.axis_size(axis)
        ends = count - 1
        head = lax.slice_in_dim(cells, 0, width, axis=dim)
        tail = lax.slice_in_dim(cells, cells.shape[dim] - width, cells.shape[dim], axis=dim)
        cells = jnp.concatenate(
            [
                lax.ppermute(tail, axis, [(i, (i + 1) % count) for i in range(ends)]),
                cells,
                lax.ppermute(head, axis, [((i + 1) % count, i) for i in range(ends)]),
            ],
            axis=dim,
        )
    return cells


def gather_batch(block, axis):
    count = lax.axis_size("batch")
    copies = jnp.broadcast_to(block[None], (count,) + block.shape)
    arrived = jnp.moveaxis(lax.all_to_all(copies, "batch", 0, 0, tiled=False), 0, axis)
    return arrived.reshape(
        block.shape[:axis] + (count * block.shape[axis],) + block.shape[axis + 1 :]
    )


def normalize(rows_in, gain):
    values = rows_in.astype(jnp.float32)
    scale = lax.rsqrt(jnp.mean(values * values, axis=-1, keepdims=True) + 1e-06)
    return values * scale * gain


def shards(
    activations,
    conv_gain,
    conv_weight,
    attention_gain,
    query_weight,
    key_weight,
    value_weight,
    output_weight,
):
    sample_count, own_rows, full_width = activations.shape
    tap_count, local_out, _ = conv_weight.shape
    flank_rows = tap_count // 2
    gathered_in = gather_batch(activations, 1)
    seq_rows = gathered_in.shape[1]
    active = jax.nn.gelu(normalize(gathered_in, conv_gain)).astype(jnp.bfloat16)
    framed = with_halo(active, (("seq", 1),), flank_rows)
    conv_sum = jnp.zeros((sample_count, local_out, seq_rows), jnp.float32)
    for offset in range(tap_count):
        conv_sum = conv_sum + jnp.einsum(
            "std,ed->set",
            framed[:, offset : offset + seq_rows],
            conv_weight[offset],
            preferred_element_type=jnp.float32,
        )
    column_start = lax.axis_index("batch") * local_out
    own_columns = lax.dynamic_slice_in_dim(gathered_in, column_start, local_out, 2)
    residual = jnp.transpose(own_columns, (0, 2, 1)).astype(jnp.float32)
    hidden_part = (residual + conv_sum).astype(jnp.bfloat16)
    hidden_full = gather_batch(hidden_part, 1)
    hidden_float = hidden_full.astype(jnp.float32)
    norm_scale = lax.rsqrt(jnp.mean(hidden_float * hidden_float, axis=1, keepdims=True) + 1e-06)
    normed = (hidden_float * norm_scale * attention_gain[None, :, None]).astype(jnp.bfloat16)
    queries = (
        jnp.einsum("sdt,ed->set", normed, query_weight, preferred_element_type=jnp.float32)
        * HD ** (-0.5)
    ).astype(jnp.bfloat16)
    key_rows = jnp.einsum(
        "sdt,ed->set", normed, key_weight, preferred_element_type=jnp.float32
    ).astype(jnp.bfloat16)
    value_rows = jnp.einsum(
        "sdt,ed->set", normed, value_weight, preferred_element_type=jnp.float32
    ).astype(jnp.bfloat16)
    heads_here = query_weight.shape[0] // HD
    query_heads = queries.reshape(sample_count, heads_here, HD, seq_rows)
    start_max = jnp.full((sample_count, heads_here, seq_rows), -jnp.inf, jnp.float32)
    start_sum = jnp.zeros((sample_count, heads_here, seq_rows), jnp.float32)
    start_acc = jnp.zeros((sample_count, heads_here, HD, seq_rows), jnp.float32)
    key_tile = lax.all_gather(key_rows, "seq", axis=2, tiled=True)
    value_tile = lax.all_gather(value_rows, "seq", axis=2, tiled=True)
    key_count = key_tile.shape[2]
    block_rows = math.gcd(key_count, 512)

    def consume(block_index, running):
        running_max, weight_sum, summed = running
        begin = block_index * block_rows
        key_block = lax.dynamic_slice_in_dim(key_tile, begin, block_rows, 2).reshape(
            sample_count, heads_here, HD, block_rows
        )
        value_block = lax.dynamic_slice_in_dim(value_tile, begin, block_rows, 2).reshape(
            sample_count, heads_here, HD, block_rows
        )
        scores = jnp.einsum(
            "shdq,shdk->shqk", query_heads, key_block, preferred_element_type=jnp.float32
        )
        new_max = jnp.maximum(running_max, jnp.max(scores, axis=-1))
        weights = jnp.exp(scores - new_max[..., None])
        rescale = jnp.exp(running_max - new_max)
        weight_sum = weight_sum * rescale + jnp.sum(weights, axis=-1)
        summed = summed * rescale[:, :, None, :] + jnp.einsum(
            "shqk,shdk->shdq",
            weights.astype(jnp.bfloat16),
            value_block,
            preferred_element_type=jnp.float32,
        )
        return (new_max, weight_sum, summed)

    final_max, weight_sum, summed = lax.fori_loop(
        0, key_count // block_rows, consume, (start_max, start_sum, start_acc)
    )
    attended = (
        (summed / weight_sum[:, :, None, :])
        .astype(jnp.bfloat16)
        .reshape(sample_count, heads_here * HD, seq_rows)
    )
    row_start = lax.axis_index("batch") * own_rows
    own_hidden = jnp.transpose(
        lax.dynamic_slice_in_dim(hidden_full, row_start, own_rows, 2), (0, 2, 1)
    ).astype(jnp.float32)
    batch_count = lax.axis_size("batch")
    partial_rows = jnp.einsum(
        "set,ef->tsf", attended, output_weight, preferred_element_type=jnp.float32
    ).astype(jnp.bfloat16)
    partial_rows = partial_rows.reshape(batch_count, own_rows, sample_count, full_width)
    share_rows = jnp.sum(
        lax.all_to_all(partial_rows, "batch", 0, 0, tiled=False).astype(jnp.float32), axis=0
    )
    branch_rows = jnp.transpose(share_rows, (1, 0, 2))
    result = own_hidden + branch_rows
    return result.astype(jnp.bfloat16)


def solution(mesh):
    placed = (
        P(None, ("seq", "batch"), None),
        P(),
        P(None, "batch", None),
        P(),
        P("batch", None),
        P("batch", None),
        P("batch", None),
        P("batch", None),
    )
    return jax.shard_map(
        shards,
        mesh=mesh,
        in_specs=placed,
        out_specs=P(None, ("seq", "batch"), None),
        check_vma=False,
    )
```

profile of v0, /device:TPU:0, one launch (start us, length us, event | category | flops | bytes accessed | tf_op | source)
XLA Modules:
  0.0 335.0 jit_solution(1888584935394674766)
XLA Ops:
  6.5 3.0 broadcast_in_dim.14
  9.6 7.0 %all-to-all-start = ((bf16[8,2,64,1536]{3,2,1,0:T(8,128)(2,1)}), bf16[8,2,64,1536]{3,2,1,0:T(8,128)(2,1)}, u32[]{:S(2)}, u32[]{:S(2)}) async-start(bf16[8,2,64,1536]{3,2,1,0:T(8,128)(2,1)} %broadcast_in_dim.14), calls=%async_computation | async-start | bytes 6291456 | tf_op jit(solution)/shard_map/all_to_all | solution.py:30
  16.6 39.8 %all-to-all-done = bf16[8,2,64,1536]{3,2,1,0:T(8,128)(2,1)} async-done(((bf16[8,2,64,1536]{3,2,1,0:T(8,128)(2,1)}), bf16[8,2,64,1536]{3,2,1,0:T(8,128)(2,1)}, u32[]{:S(2)}, u32[]{:S(2)}) %all-to-all-start) | async-done | bytes 3145760 | tf_op jit(solution)/shard_map/all_to_all | solution.py:30
  56.4 2.6 fusion.13
  59.1 2.2 copy.63
  61.3 3.0 fusion.29
  65.6 4.2 %fusion.17 = bf16[2,8,64,1536]{3,2,1,0:T(8,128)(2,1)S(1)} fusion(f32[1536]{0:T(1024)S(1)} %copy-done.5, f32[2,8,64]{2,1,0:T(8,128)S(1)} %add_rsqrt_fusion, bf16[8,2,64,1536]{3,2,1,0:T(8,128)(2,1)} %all-to-all-done), kind=kLoop, calls=%fused_computation.29 | loop fusion | flops 18874368 | bytes 6301696 | tf_op jit(solution)/shard_map/convert_element_type | solution.py:57
  69.8 2.2 fusion.73
  72.5 3.3 collective-permute-start
  75.9 3.2 fusion.32
  83.1 43.2 %all_to_all.15 = bf16[8,2,192,512]{3,2,1,0:T(8,128)(2,1)S(1)} all-to-all(bf16[8,2,192,512]{3,2,1,0:T(8,128)(2,1)S(1)} %broadcast_in_dim.15), channel_id=1, replica_groups=mesh['seq'=16,'batch'=8] {'batch'}, dimensions={0} | all-to-all | bytes 6291456 | tf_op jit(solution)/shard_map/all_to_all | solution.py:30
  129.3 1.6 copy-done.4
  130.9 1.5 fusion.60
  132.5 3.5 %fusion.61 = bf16[2,192,512]{2,1,0:T(8,128)(2,1)} fusion(bf16[2,1536,512]{2,1,0:T(8,128)(2,1)} %copy-done.4, bf16[192,1536]{1,0:T(8,128)(2,1)S(1)} %copy-done.9), kind=kOutput, calls=%fused_computation.72 | convolution fusion | flops 604176384 | bytes 4128768 | tf_op jit(solution)/shard_map/sdt,ed->set/dot_general | solution.py:82
  136.1 2.7 fusion.62
  138.7 34.8 %all-gather.3.cloned.1.call-done = bf16[2,192,8192]{2,1,0:T(8,128)(2,1)} async-done(((bf16[2,192,512]{2,1,0:T(8,128)(2,1)}), bf16[2,192,8192]{2,1,0:T(8,128)(2,1)}) %all-gather.3.cloned.1.call-update) | async-done | bytes 6291472 | tf_op jit(solution)/shard_map/all_gather | solution.py:90
  173.6 45.0 %all-gather.5.cloned.1.call-done = bf16[2,192,8192]{2,1,0:T(8,128)(2,1)} async-done(((bf16[2,192,512]{2,1,0:T(8,128)(2,1)}), bf16[2,192,8192]{2,1,0:T(8,128)(2,1)}) %all-gather.5.cloned.1.call-update) | async-done | bytes 6291472 | tf_op jit(solution)/shard_map/all_gather | solution.py:91
  218.5 56.6 %while.18 = (s32[]{:T(128)}, f32[2,1,512]{2,0,1:T(2,128)S(1)}, f32[2,1,512]{2,0,1:T(2,128)S(1)}, f32[2,1,192,512]{3,2,0,1:T(8,128)S(1)}, bf16[2,192,8192]{2,1,0:...) while((s32[]{:T(128)}, f32[2,1,512]{2,0,1:T(2,128)S(1)}, ...), condition=%wide.region_5.0_spmd.clone, body=%wide.region_2.0_spmd.clone.sunk | while | flops 405870592 | bytes 9109687 | solution.py:119
  220.4 1.6 fusion.101
  223.9 1.6 fusion.101
  225.6 1.5 bitcast_reduce_fusion.2
  227.4 1.6 fusion.101
  229.1 1.5 bitcast_reduce_fusion.2
  231.0 1.6 fusion.101
  234.5 1.6 fusion.101
  236.2 1.5 bitcast_reduce_fusion.2
  238.0 1.6 fusion.101
  239.7 1.5 bitcast_reduce_fusion.2
  241.6 1.6 fusion.101
  243.3 1.5 bitcast_reduce_fusion.2
  245.1 1.6 fusion.101
  246.8 1.5 bitcast_reduce_fusion.2
  248.7 1.6 fusion.101
  250.4 1.5 bitcast_reduce_fusion.2
  252.2 1.6 fusion.101
  253.9 1.5 bitcast_reduce_fusion.2
  255.7 1.6 fusion.101
  257.4 1.5 bitcast_reduce_fusion.2
  259.3 1.6 fusion.101
  261.0 1.5 bitcast_reduce_fusion.2
  262.8 1.6 fusion.101
  266.3 1.6 fusion.101
  269.9 1.6 fusion.101
  273.4 1.6 fusion.101
  276.1 2.0 copy.67
  278.1 6.6 %all-to-all-start.2 = ((bf16[8,64,2,1536]{3,1,2,0:T(8,128)(2,1)}), bf16[8,64,2,1536]{3,1,2,0:T(8,128)(2,1)}, u32[]{:S(2)}, u32[]{:S(2)}) async-start(bf16[8,64,2,1536]{3,1,2,0:T(8,128)(2,1)} %copy.67), calls=%async_computation.2 | async-start | bytes 6291456 | tf_op jit(solution)/shard_map/all_to_all | solution.py:137
  286.4 38.6 %all-to-all-done.2 = bf16[8,64,2,1536]{3,1,2,0:T(8,128)(2,1)} async-done(((bf16[8,64,2,1536]{3,1,2,0:T(8,128)(2,1)}), bf16[8,64,2,1536]{3,1,2,0:T(8,128)(2,1)}, u32[]{:S(2)}, u32[]{:S(2)}) %all-to-all-start.2) | async-done | bytes 3145760 | tf_op jit(solution)/shard_map/all_to_all | solution.py:137
  324.9 2.4 convert_reduce_fusion
  (118 shorter events, 26.8 us)
Async XLA Ops:
  6.5 268.6 %copy-start = (bf16[192,1536]{1,0:T(8,128)(2,1)S(1)}, bf16[192,1536]{1,0:T(8,128)(2,1)}, u32[]{:S(2)}) copy-start(bf16[192,1536]{1,0:T(8,128)(2,1)} %param.17) | copy-start | bytes 1769476
  9.6 46.8 %all-to-all-start = ((bf16[8,2,64,1536]{3,2,1,0:T(8,128)(2,1)}), bf16[8,2,64,1536]{3,2,1,0:T(8,128)(2,1)}, u32[]{:S(2)}, u32[]{:S(2)}) async-start(bf16[8,2,64,1536]{3,2,1,0:T(8,128)(2,1)} %broadcast_in_dim.14), calls=%async_computation | async-start | bytes 6291456 | tf_op jit(solution)/shard_map/all_to_all | solution.py:30
  16.6 157.0 %all-gather.3.cloned.1.call-start = ((), (), s32[]{:S(2)}) async-start(), calls=%async_computation.3 | async-start | bytes 6684672 | tf_op jit(solution)/shard_map/all_gather | solution.py:90
  59.1 2.2 copy-start.5
  64.3 5.6 %copy-start.2 = (bf16[2,512,1536]{2,1,0:T(8,128)(2,1)}, bf16[2,512,1536]{2,1,0:T(8,128)(2,1)S(1)}, u32[]{:S(2)}) copy-start(bf16[2,512,1536]{2,1,0:T(8,128)(2,1)S(1)} %fusion.29) | copy-start | bytes 9437188
  64.3 11.5 %collective-permute-start.1 = (bf16[2,2,1536]{2,1,0:T(2,128)(2,1)S(1)}, bf16[2,2,1536]{2,1,0:T(2,128)(2,1)S(1)}, u32[]{:S(2)}, u32[]{:S(2)}) collective-permute-start(bf16[2,2,1536]{2,1,0:T(2,128)(2,1)S(1)} %get-tuple-element.175), channel_id=1, source_target_pairs={{8,0},{16,8},{24,16},{32,24},{40,32},{48,40},{56,48},{64,56},{72,6... | collective-permute-start | bytes 36872 | tf_op jit(solution)/shard_map/ppermute | solution.py:20
  72.5 6.5 %copy-start.3 = (bf16[2,512,1536]{2,1,0:T(8,128)(2,1)S(1)}, bf16[2,512,1536]{2,1,0:T(8,128)(2,1)}, u32[]{:S(2)}) copy-start(bf16[2,512,1536]{2,1,0:T(8,128)(2,1)} %copy-done.2) | copy-start | bytes 9437188
  72.5 6.5 %copy-start.7 = (bf16[5,192,1536]{2,1,0:T(8,128)(2,1)S(1)}, bf16[5,192,1536]{2,1,0:T(8,128)(2,1)}, u32[]{:S(2)}) copy-start(bf16[5,192,1536]{2,1,0:T(8,128)(2,1)} %param.12) | copy-start | bytes 8847364
  72.5 7.7 %collective-permute-start = (bf16[2,2,1536]{2,1,0:T(2,128)(2,1)S(1)}, bf16[2,2,1536]{2,1,0:T(2,128)(2,1)S(1)}, u32[]{:S(2)}, u32[]{:S(2)}) collective-permute-start(bf16[2,2,1536]{2,1,0:T(2,128)(2,1)S(1)} %get-tuple-element.174), channel_id=1, source_target_pairs={{0,8},{8,16},{16,24},{24,32},{32,40},{40,48},{48,56},{56,64},{64,7... | collective-permute-start | bytes 36872 | tf_op jit(solution)/shard_map/ppermute | solution.py:18
  126.9 0.7 copy-start.6
  127.6 1.6 copy-start.1
  127.6 3.3 copy-start.8
  129.3 1.6 copy-start.4
  130.9 1.6 copy-start.9
  132.5 3.6 %copy-start.10 = (bf16[192,1536]{1,0:T(8,128)(2,1)S(1)}, bf16[192,1536]{1,0:T(8,128)(2,1)}, u32[]{:S(2)}) copy-start(bf16[192,1536]{1,0:T(8,128)(2,1)} %param.14) | copy-start | bytes 1769476
  132.5 86.0 %all-gather.5.cloned.1.call-start = ((), (), s32[]{:S(2)}) async-start(), calls=%async_computation.4 | async-start | bytes 6684672 | tf_op jit(solution)/shard_map/all_gather | solution.py:91
  278.1 46.8 %all-to-all-start.2 = ((bf16[8,64,2,1536]{3,1,2,0:T(8,128)(2,1)}), bf16[8,64,2,1536]{3,1,2,0:T(8,128)(2,1)}, u32[]{:S(2)}, u32[]{:S(2)}) async-start(bf16[8,64,2,1536]{3,1,2,0:T(8,128)(2,1)} %copy.67), calls=%async_computation.2 | async-start | bytes 6291456 | tf_op jit(solution)/shard_map/all_to_all | solution.py:137
Sparse Core Ops, SparseCore 0:
  132.6 40.9 all-gather.2
  175.2 43.2 all-gather.4
where the time goes:
time: 337 us; the launch traced here: 335 us
  waiting for transfers between devices  158 us (47%)
  matrix products  68.1 us (20%)
  blocking collectives  43.2 us (13%)
  other arithmetic  19.8 us (6%)
  starting transfers between devices  18.3 us (5%)
  between operations  13.7 us (4%)
  local copies, waits for them, and re-layouts  12.9 us (4%)
    all_gather x1, waiting for transfers between devices, shards(): value_tile = lax.all_gather(value_rows, 'seq', axis=2, tiled=True)  45 us
    all_to_all x1, blocking collectives, gather_batch(): lax.all_to_all(copies, 'batch', 0, 0, tiled=False)  43.2 us
    all_to_all x1, waiting for transfers between devices, gather_batch(): lax.all_to_all(copies, 'batch', 0, 0, tiled=False)  39.8 us
    all_to_all x1, waiting for transfers between devices, shards(): lax.all_to_all(partial_rows, 'batch', 0, 0, tiled=False).astype(jnp.float32)  38.6 us
    all_gather x1, waiting for transfers between devices, shards(): key_tile = lax.all_gather(key_rows, 'seq', axis=2, tiled=True)  34.8 us
    dot_general x16, matrix products, consume(): jnp.einsum('shqk,shdk->shdq', weights.astype(jnp.bfloat16), value_block,...  26.3 us
    dot_general x16, matrix products, consume(): jnp.einsum('shdq,shdk->shqk', query_heads, key_block, preferred_element_t...  24 us
    dot_general x5, matrix products, shards(): jnp.einsum('std,ed->set', framed[:, offset:offset + seq_rows], conv_weigh...  9.08 us
  transfers between devices with their start and end apart: 6, of which 4 were waited for; matrix products, arithmetic and copies ran while one was open for 6% of the time, Pallas kernels for 0%

commit v1 on v0

--- a/solution.py
+++ b/solution.py
@@ -87,7 +87,8 @@
     start_max = jnp.full((sample_count, heads_here, seq_rows), -jnp.inf, jnp.float32)
     start_sum = jnp.zeros((sample_count, heads_here, seq_rows), jnp.float32)
     start_acc = jnp.zeros((sample_count, heads_here, HD, seq_rows), jnp.float32)
-    key_tile = lax.all_gather(key_rows, "seq", axis=2, tiled=True)
+    stack = jnp.stack([key_rows] * lax.axis_size("seq"))
+    key_tile = jnp.concatenate(lax.all_to_all(stack, "seq", 0, 0), axis=2)
     value_tile = lax.all_gather(value_rows, "seq", axis=2, tiled=True)
     key_count = key_tile.shape[2]
     block_rows = math.gcd(key_count, 512)

time: 337 us -> 378 us (1.12)
  waiting for transfers between devices: 158 us -> 181 us
  local copies, waits for them, and re-layouts: 12.9 us -> 23.2 us
  starting transfers between devices: 18.3 us -> 24.6 us
    all_to_all x0 -> x1, waiting for transfers between devices: none -> 103 us  [shards(): key_tile = jnp.concatenate(lax.all_to_all(stack, 'seq', 0, 0), axis=2)]
    all_gather x1, waiting for transfers between devices: 45 us -> 0.01 us  [shards(): value_tile = lax.all_gather(value_rows, 'seq', axis=2, tiled=True)]
    all_gather x1 -> x0, waiting for transfers between devices: 34.8 us -> none  [shards(): key_tile = lax.all_gather(key_rows, 'seq', axis=2, tiled=True)]
    all_to_all x0 -> x1, starting transfers between devices: none -> 8.54 us  [shards(): key_tile = jnp.concatenate(lax.all_to_all(stack, 'seq', 0, 0), axis=2)]
    reshape x0 -> x1, local copies, waits for them, and re-layouts: none -> 6.34 us  [shards(): key_tile = jnp.concatenate(lax.all_to_all(stack, 'seq', 0, 0), axis=2)]
  transfers between devices with their start and end apart: 6 -> 6, of which waited for: 4 -> 3; matrix products, arithmetic and copies ran while one was open for 6% -> 8% of each run, Pallas kernels for 0% -> 0%
where the time goes in v1:
time: 378 us; the launch traced here: 376 us
  waiting for transfers between devices  181 us (48%)
  matrix products  70.2 us (19%)
  blocking collectives  42.5 us (11%)
  starting transfers between devices  24.6 us (7%)
  local copies, waits for them, and re-layouts  23.2 us (6%)
  other arithmetic  19.8 us (5%)
  between operations  13.7 us (4%)
    all_to_all x1, waiting for transfers between devices, shards(): key_tile = jnp.concatenate(lax.all_to_all(stack, 'seq', 0, 0), axis=2)  103 us
    all_to_all x1, blocking collectives, gather_batch(): lax.all_to_all(copies, 'batch', 0, 0, tiled=False)  42.5 us
    all_to_all x1, waiting for transfers between devices, gather_batch(): lax.all_to_all(copies, 'batch', 0, 0, tiled=False)  39.8 us
    all_to_all x1, waiting for transfers between devices, shards(): lax.all_to_all(partial_rows, 'batch', 0, 0, tiled=False).astype(jnp.float32)  38.2 us
    dot_general x16, matrix products, consume(): jnp.einsum('shqk,shdk->shdq', weights.astype(jnp.bfloat16), value_block,...  26.3 us
    dot_general x16, matrix products, consume(): jnp.einsum('shdq,shdk->shqk', query_heads, key_block, preferred_element_t...  26 us
    dot_general x5, matrix products, shards(): jnp.einsum('std,ed->set', framed[:, offset:offset + seq_rows], conv_weigh...  9.23 us
    all_to_all x1, starting transfers between devices, shards(): key_tile = jnp.concatenate(lax.all_to_all(stack, 'seq', 0, 0), axis=2)  8.54 us
  transfers between devices with their start and end apart: 6, of which 3 were waited for; matrix products, arithmetic and copies ran while one was open for 8% of the time, Pallas kernels for 0%

profile of v1, /device:TPU:0, one launch (start us, length us, event | category | flops | bytes accessed | tf_op | source)
XLA Modules:
  0.0 376.3 jit_solution(10111257264327265974)
XLA Ops:
  6.5 3.0 broadcast_in_dim.14
  9.6 7.0 %all-to-all-start = ((bf16[8,2,64,1536]{3,2,1,0:T(8,128)(2,1)}), bf16[8,2,64,1536]{3,2,1,0:T(8,128)(2,1)}, u32[]{:S(2)}, u32[]{:S(2)}) async-start(bf16[8,2,64,1536]{3,2,1,0:T(8,128)(2,1)} %broadcast_in_dim.14), calls=%async_computation | async-start | bytes 6291456 | tf_op jit(solution)/shard_map/all_to_all | solution.py:30
  16.6 39.8 %all-to-all-done = bf16[8,2,64,1536]{3,2,1,0:T(8,128)(2,1)} async-done(((bf16[8,2,64,1536]{3,2,1,0:T(8,128)(2,1)}), bf16[8,2,64,1536]{3,2,1,0:T(8,128)(2,1)}, u32[]{:S(2)}, u32[]{:S(2)}) %all-to-all-start) | async-done | bytes 3145760 | tf_op jit(solution)/shard_map/all_to_all | solution.py:30
  56.4 2.6 fusion.13
  59.1 2.2 copy.65
  61.3 3.0 fusion.29
  66.9 4.2 %fusion.17 = bf16[2,8,64,1536]{3,2,1,0:T(8,128)(2,1)S(1)} fusion(f32[1536]{0:T(1024)S(1)} %copy-done.5, f32[2,8,64]{2,1,0:T(8,128)S(1)} %add_rsqrt_fusion, bf16[8,2,64,1536]{3,2,1,0:T(8,128)(2,1)} %all-to-all-done), kind=kLoop, calls=%fused_computation.29 | loop fusion | flops 18874368 | bytes 6301696 | tf_op jit(solution)/shard_map/convert_element_type | solution.py:57
  71.1 2.2 fusion.73
  73.8 3.4 fusion.32
  81.7 42.5 %all_to_all.20 = bf16[8,2,192,512]{3,2,1,0:T(8,128)(2,1)S(1)} all-to-all(bf16[8,2,192,512]{3,2,1,0:T(8,128)(2,1)S(1)} %broadcast_in_dim.15), channel_id=1, replica_groups=mesh['seq'=16,'batch'=8] {'batch'}, dimensions={0} | all-to-all | bytes 6291456 | tf_op jit(solution)/shard_map/all_to_all | solution.py:30
  127.3 1.6 copy-done.4
  130.5 2.7 fusion.60
  133.2 3.4 stack.2
  136.5 8.5 %all-to-all-start.2 = ((bf16[16,2,192,512]{3,2,1,0:T(8,128)(2,1)}), bf16[16,2,192,512]{3,2,1,0:T(8,128)(2,1)}, u32[]{:S(2)}, u32[]{:S(2)}) async-start(bf16[16,2,192,512]{3,2,1,0:T(8,128)(2,1)} %stack.2), calls=%async_computation.2 | async-start | bytes 12582912 | tf_op jit(solution)/shard_map/all_to_all | solution.py:91
  145.1 3.5 fusion.62
  148.6 103.4 %all-to-all-done.2 = bf16[16,2,192,512]{3,2,1,0:T(8,128)(2,1)} async-done(((bf16[16,2,192,512]{3,2,1,0:T(8,128)(2,1)}), bf16[16,2,192,512]{3,2,1,0:T(8,128)(2,1)}, u32[]{:S(2)}, u32[]{:S(2)}) %all-to-all-start.2) | async-done | bytes 6291488 | tf_op jit(solution)/shard_map/all_to_all | solution.py:91
  252.0 6.3 %copy.76 = bf16[16,2,24,8,512]{4,3,0,2,1:T(8,128)(2,1)} copy(bf16[16,2,24,8,512]{4,3,2,1,0:T(8,128)(2,1)} %bitcast.42) | data formatting | bytes 12582912 | tf_op jit(solution)/shard_map/reshape | solution.py:91
  258.4 58.6 %while.18 = (s32[]{:T(128)}, f32[2,1,512]{2,0,1:T(2,128)S(1)}, f32[2,1,512]{2,0,1:T(2,128)S(1)}, f32[2,1,192,512]{3,2,0,1:T(8,128)S(1)}, bf16[2,192,8192]{2,1,0:...) while((s32[]{:T(128)}, f32[2,1,512]{2,0,1:T(2,128)S(1)}, ...), condition=%wide.region_5.0_spmd.clone, body=%wide.region_2.0_spmd.clone.sunk | while | flops 405870592 | bytes 9109679 | solution.py:120
  260.0 1.6 fusion.101
  263.7 1.6 fusion.101
  265.7 1.6 bitcast_reduce_fusion.2
  267.3 1.6 fusion.101
  269.3 1.6 bitcast_reduce_fusion.2
  271.0 1.6 fusion.101
  273.0 1.6 bitcast_reduce_fusion.2
  274.7 1.6 fusion.101
  278.3 1.6 fusion.101
  280.3 1.6 bitcast_reduce_fusion.2
  282.0 1.6 fusion.101
  284.0 1.6 bitcast_reduce_fusion.2
  285.6 1.6 fusion.101
  287.6 1.6 bitcast_reduce_fusion.2
  289.3 1.6 fusion.101
  293.0 1.6 fusion.101
  295.0 1.6 bitcast_reduce_fusion.2
  296.6 1.6 fusion.101
  298.6 1.6 bitcast_reduce_fusion.2
  300.3 1.6 fusion.101
  303.9 1.6 fusion.101
  307.6 1.6 fusion.101
  309.6 1.6 bitcast_reduce_fusion.2
  311.3 1.6 fusion.101
  313.3 1.6 bitcast_reduce_fusion.2
  314.9 1.6 fusion.101
  318.0 2.0 copy.70
  319.9 6.4 %all-to-all-start.3 = ((bf16[8,64,2,1536]{3,1,2,0:T(8,128)(2,1)}), bf16[8,64,2,1536]{3,1,2,0:T(8,128)(2,1)}, u32[]{:S(2)}, u32[]{:S(2)}) async-start(bf16[8,64,2,1536]{3,1,2,0:T(8,128)(2,1)} %copy.70), calls=%async_computation.3 | async-start | bytes 6291456 | tf_op jit(solution)/shard_map/all_to_all | solution.py:138
  328.0 38.2 %all-to-all-done.3 = bf16[8,64,2,1536]{3,1,2,0:T(8,128)(2,1)} async-done(((bf16[8,64,2,1536]{3,1,2,0:T(8,128)(2,1)}), bf16[8,64,2,1536]{3,1,2,0:T(8,128)(2,1)}, u32[]{:S(2)}, u32[]{:S(2)}) %all-to-all-start.3) | async-done | bytes 3145760 | tf_op jit(solution)/shard_map/all_to_all | solution.py:138
  366.2 2.4 convert_reduce_fusion
  (119 shorter events, 30.9 us)
Async XLA Ops:
  6.5 310.4 %copy-start = (bf16[192,1536]{1,0:T(8,128)(2,1)S(1)}, bf16[192,1536]{1,0:T(8,128)(2,1)}, u32[]{:S(2)}) copy-start(bf16[192,1536]{1,0:T(8,128)(2,1)} %param.17) | copy-start | bytes 1769476
  9.6 46.8 %all-to-all-start = ((bf16[8,2,64,1536]{3,2,1,0:T(8,128)(2,1)}), bf16[8,2,64,1536]{3,2,1,0:T(8,128)(2,1)}, u32[]{:S(2)}, u32[]{:S(2)}) async-start(bf16[8,2,64,1536]{3,2,1,0:T(8,128)(2,1)} %broadcast_in_dim.14), calls=%async_computation | async-start | bytes 6291456 | tf_op jit(solution)/shard_map/all_to_all | solution.py:30
  16.6 241.8 %all-gather.2.cloned.1.call-start = ((), (), s32[]{:S(2)}) async-start(), calls=%async_computation.4 | async-start | bytes 6684672 | tf_op jit(solution)/shard_map/all_gather | solution.py:92
  59.1 2.2 copy-start.5
  64.3 6.8 %copy-start.2 = (bf16[2,512,1536]{2,1,0:T(8,128)(2,1)}, bf16[2,512,1536]{2,1,0:T(8,128)(2,1)S(1)}, u32[]{:S(2)}) copy-start(bf16[2,512,1536]{2,1,0:T(8,128)(2,1)S(1)} %fusion.29) | copy-start | bytes 9437188
  64.3 14.6 %collective-permute-start = (bf16[2,2,1536]{2,1,0:T(2,128)(2,1)S(1)}, bf16[2,2,1536]{2,1,0:T(2,128)(2,1)S(1)}, u32[]{:S(2)}, u32[]{:S(2)}) collective-permute-start(bf16[2,2,1536]{2,1,0:T(2,128)(2,1)S(1)} %get-tuple-element.174), channel_id=1, source_target_pairs={{0,8},{8,16},{16,24},{24,32},{32,40},{40,48},{48,56},{56,64},{64,7... | collective-permute-start | bytes 36872 | tf_op jit(solution)/shard_map/ppermute | solution.py:18
  65.6 8.2 %collective-permute-start.1 = (bf16[2,2,1536]{2,1,0:T(2,128)(2,1)S(1)}, bf16[2,2,1536]{2,1,0:T(2,128)(2,1)S(1)}, u32[]{:S(2)}, u32[]{:S(2)}) collective-permute-start(bf16[2,2,1536]{2,1,0:T(2,128)(2,1)S(1)} %get-tuple-element.175), channel_id=1, source_target_pairs={{8,0},{16,8},{24,16},{32,24},{40,32},{48,40},{56,48},{64,56},{72,6... | collective-permute-start | bytes 36872 | tf_op jit(solution)/shard_map/ppermute | solution.py:20
  73.8 3.4 copy-start.3
  73.8 3.9 %copy-start.7 = (bf16[5,192,1536]{2,1,0:T(8,128)(2,1)S(1)}, bf16[5,192,1536]{2,1,0:T(8,128)(2,1)}, u32[]{:S(2)}) copy-start(bf16[5,192,1536]{2,1,0:T(8,128)(2,1)} %param.12) | copy-start | bytes 8847364
  124.9 0.7 copy-start.6
  125.6 1.7 copy-start.1
  125.6 3.3 copy-start.8
  127.3 1.7 copy-start.4
  128.9 1.6 copy-start.9
  136.5 8.6 %copy-start.10 = (bf16[192,1536]{1,0:T(8,128)(2,1)S(1)}, bf16[192,1536]{1,0:T(8,128)(2,1)}, u32[]{:S(2)}) copy-start(bf16[192,1536]{1,0:T(8,128)(2,1)} %param.14) | copy-start | bytes 1769476
  136.5 115.5 %all-to-all-start.2 = ((bf16[16,2,192,512]{3,2,1,0:T(8,128)(2,1)}), bf16[16,2,192,512]{3,2,1,0:T(8,128)(2,1)}, u32[]{:S(2)}, u32[]{:S(2)}) async-start(bf16[16,2,192,512]{3,2,1,0:T(8,128)(2,1)} %stack.2), calls=%async_computation.2 | async-start | bytes 12582912 | tf_op jit(solution)/shard_map/all_to_all | solution.py:91
  319.9 46.3 %all-to-all-start.3 = ((bf16[8,64,2,1536]{3,1,2,0:T(8,128)(2,1)}), bf16[8,64,2,1536]{3,1,2,0:T(8,128)(2,1)}, u32[]{:S(2)}, u32[]{:S(2)}) async-start(bf16[8,64,2,1536]{3,1,2,0:T(8,128)(2,1)} %copy.70), calls=%async_computation.3 | async-start | bytes 6291456 | tf_op jit(solution)/shard_map/all_to_all | solution.py:138
Sparse Core Ops, SparseCore 0:
  130.6 110.7 all-gather.1
